TPU v7x, 128 devices: a whole 4x4x4 slice. The times are simulated.
128 devices in a mesh: dp: 8 (over x, core), eig: 16 (over y, z).
Axes of the slice: x: 4, y: 4, z: 4, core: 2. Of those that a mesh axis runs over, the one named last changes fastest.
Arguments:
- acts: bfloat16 [4096, 8192], P(('dp', 'eig')), may hold values from -6 to 6
- grads: bfloat16 [4096, 8192], P(('dp', 'eig')), may hold values from -6 to 6
- act_basis: bfloat16 [4096, 8192], P('eig'), may hold values from -0.0625 to 0.0625
- grad_basis: bfloat16 [4096, 8192], P('eig'), may hold values from -0.0625 to 0.0625
- eigenvalues: float32 [4096, 4096], P('eig'), may hold values from 0.05 to 20
- query_grads: bfloat16 [32, 256, 4096], P('dp', None, 'eig'), may hold values from -6 to 6
- query_acts: bfloat16 [32, 256, 4096], P('dp'), may hold values from -6 to 6
- cand_local: int32 [8, 16], P('dp'), may hold values from 0 to 7, as said below
- seq_lengths: int32 [8, 8], P('dp'), may hold values from 1 to 128, 512 in all within a row
Outputs:
- scores: float32 [32, 16], P('dp')
Inputs may be any that keep to these rules, and one draw needn't show every extreme that they name: `cand_local`: entry j of an owner's list names a sequence of dp shard j // 2; the 2 entries of one list that name one shard differ. `seq_lengths`: row d lists the lengths of the 8 sequences packed in order in dp shard d's 512 token rows; they sum to 512.
All inputs are finite; a program needn't handle non-finite values.
Results may differ from a plain program's by a relative error of at most 0.006.
Values may be sent and summed in bfloat16 or wider, within the bound.
No kernel may reach another device: no remote copies, remote signals or barrier semaphores. Data moves between devices by JAX's collectives and lax.ppermute only.
A program may use at most 128 MiB of HBM per device.

v0:
```python
import math

import jax
import jax.numpy as jnp
from jax import lax
from jax.sharding import PartitionSpec as P

DAMPING = 0.1


def shards(
    acts,
    grads,
    act_basis,
    grad_basis,
    eigenvalues,
    query_grads,
    query_acts,
    cand_local,
    seq_lengths,
):
    block_width = act_basis.shape[0]
    stacked = jnp.stack([acts, grads])
    shard_rows = lax.all_gather(stacked, "eig", axis=1, tiled=True)
    act_part = jnp.dot(shard_rows[0], act_basis.T, preferred_element_type=jnp.float32)
    grad_part = jnp.dot(shard_rows[1], grad_basis.T, preferred_element_type=jnp.float32)
    rotated = jnp.concatenate([act_part, grad_part], axis=1).astype(jnp.bfloat16)
    act_block = rotated[:, :block_width]
    grad_block = rotated[:, block_width:]
    group_rows = rotated.shape[0]
    seq_count = seq_lengths.shape[1]
    max_len = 2 * group_rows // seq_count
    pick_lists = lax.all_to_all(cand_local, "dp", split_axis=1, concat_axis=0, tiled=True)
    owners = pick_lists.shape[0]
    per_shard = pick_lists.shape[1]
    lengths = seq_lengths[0]
    offsets = jnp.cumsum(lengths) - lengths
    chosen = (
        pick_lists[:, :, None] == jnp.arange(seq_count, dtype=jnp.int32)[None, None, :]
    ).astype(jnp.int32)
    pick_len = jnp.sum(chosen * lengths[None, None, :], axis=2)
    pick_start = jnp.sum(chosen * offsets[None, None, :], axis=2)
    within = jnp.arange(max_len, dtype=jnp.int32)
    is_live = within[None, None, :] < pick_len[:, :, None]
    row_index = jnp.where(is_live, pick_start[:, :, None] + within[None, None, :], 0).reshape(-1)
    live_rows = is_live.reshape(owners, per_shard * max_len, 1)

    def pack_rows(source):
        gathered_rows = jnp.take(source, row_index, axis=0).reshape(
            owners, per_shard * max_len, source.shape[1]
        )
        return jnp.where(live_rows, gathered_rows, jnp.zeros((), jnp.bfloat16))

    grad_pack = pack_rows(grad_block)
    grad_recv, act_narrow = (
        lax.all_to_all(grad_pack, "dp", split_axis=0, concat_axis=0, tiled=True),
        lax.all_to_all(pack_rows(act_block), "dp", split_axis=0, concat_axis=0, tiled=True),
    )
    act_recv = lax.all_gather(act_narrow, "eig", axis=2, tiled=True)
    slot_count = owners * per_shard * max_len
    full_width = query_acts.shape[2]
    grad_flat = grad_recv.reshape(slot_count, block_width).astype(jnp.float32)
    act_flat = act_recv.reshape(slot_count, full_width)
    damped = eigenvalues + DAMPING

    def score_query(query_pair):
        query_grad, query_act = query_pair
        query_outer = jnp.dot(query_grad.T, query_act, preferred_element_type=jnp.float32)
        precond = (query_outer / damped).astype(jnp.bfloat16)
        projected = lax.dot_general(
            act_flat, precond, (((1,), (1,)), ((), ())), preferred_element_type=jnp.float32
        )
        per_token = jnp.sum(projected * grad_flat, axis=1)
        return jnp.sum(per_token.reshape(owners * per_shard, max_len), axis=1)

    partial_sums = lax.map(score_query, (query_grads, query_acts))
    summed = lax.psum(partial_sums, "eig")
    score_scale = 1.0 / (full_width * 4.0 * math.sqrt(query_acts.shape[1]))
    return summed * score_scale


def solution(mesh):
    placed = (
        P(("dp", "eig"), None),
        P(("dp", "eig"), None),
        P("eig", None),
        P("eig", None),
        P("eig", None),
        P("dp", None, "eig"),
        P("dp", None, None),
        P("dp", None),
        P("dp", None),
    )
    return jax.shard_map(
        shards, mesh=mesh, in_specs=placed, out_specs=P("dp", None), check_vma=False
    )
```

profile of v0, /device:TPU:0, one launch (start us, length us, event | category | flops | bytes accessed | tf_op | source)
XLA Modules:
  0.0 384.3 jit_solution(13105366813927029866)
XLA Ops:
  6.5 0.0 all-gather.3.cloned.1.call-start
  6.5 2.3 pad_maximum_fusion
  8.8 0.0 all-gather.3.cloned.1.call-update
  8.9 0.5 broadcast.35
  9.4 1.3 reduce.3
  10.7 0.7 all_to_all.16
  11.4 4.4 %all-to-all-start = ((s32[1,8,2]{2,0,1:T(1,128)}), s32[1,8,2]{2,0,1:T(1,128)S(1)}, u32[]{:S(2)}, u32[]{:S(2)}) async-start(s32[1,8,2]{2,0,1:T(1,128)} %bitcast.6), calls=%async_computation | async-start | bytes 8192 | tf_op jit(solution)/shard_map/all_to_all | solution.py:33
  15.8 0.0 all-gather.5.cloned.1.call-start
  15.8 0.8 reduce-window.8
  16.7 0.7 bitcast_subtract_fusion
  17.3 3.7 all-to-all-done
  21.1 0.1 copy.21
  21.1 0.9 select_reduce_fusion.1
  22.0 0.1 copy.22
  22.1 0.1 copy.23
  22.2 0.1 broadcast_bitcast_fusion
  22.3 101.1 %all-gather.3.cloned.1.call-done = bf16[2,512,8192]{2,1,0:T(8,128)(2,1)} async-done(((bf16[2,32,8192]{2,1,0:T(8,128)(2,1)}), bf16[2,512,8192]{2,1,0:T(8,128)(2,1)}) %all-gather.3.cloned.1.call-update) | async-done | bytes 16777232 | tf_op jit(solution)/shard_map/all_gather | solution.py:24
  123.4 6.9 %fusion.17 = bf16[512,256]{1,0:T(8,128)(2,1)S(1)} fusion(bf16[256,8192]{1,0:T(8,128)(2,1)} %param.15, bf16[2,512,8192]{2,1,0:T(8,128)(2,1)} %all-gather.3.cloned.1.call-done), kind=kOutput, calls=%fused_computation.18 | convolution fusion | flops 2147614720 | bytes 12845056 | tf_op jit(solution)/shard_map/dot_general | solution.py:25
  130.3 7.5 %gather_fusion = bf16[2048,256]{1,0:T(8,128)(2,1)S(1)} fusion(bf16[512,256]{1,0:T(8,128)(2,1)S(1)} %fusion.17, s32[2048]{0:T(1024)S(1)} %fusion.19), kind=kCustom, calls=%fused_computation.clone | custom fusion | bytes 2105344 | tf_op jit(solution)/shard_map/jit(_take)/gather | solution.py:49
  137.8 6.9 %fusion.18 = bf16[512,256]{1,0:T(8,128)(2,1)S(1)} fusion(bf16[256,8192]{1,0:T(8,128)(2,1)} %param.16, bf16[2,512,8192]{2,1,0:T(8,128)(2,1)} %all-gather.3.cloned.1.call-done), kind=kOutput, calls=%fused_computation.19 | convolution fusion | flops 2147614720 | bytes 12845056 | tf_op jit(solution)/shard_map/dot_general | solution.py:26
  144.8 7.5 %gather_fusion.1 = bf16[2048,256]{1,0:T(8,128)(2,1)S(1)} fusion(bf16[512,256]{1,0:T(8,128)(2,1)S(1)} %fusion.18, s32[2048]{0:T(1024)S(1)} %fusion.19), kind=kCustom, calls=%fused_computation.1.clone | custom fusion | bytes 2105344 | tf_op jit(solution)/shard_map/jit(_take)/gather | solution.py:49
  152.3 0.5 broadcast_select_fusion
  152.7 1.3 broadcast_select_fusion.2
  154.0 20.1 %all_to_all.23 = bf16[8,256,256]{2,1,0:T(8,128)(2,1)} all-to-all(bf16[8,256,256]{2,1,0:T(8,128)(2,1)S(1)} %get-tuple-element.63), channel_id=1, replica_groups=mesh['dp'=8,'eig'=16] {'dp'}, dimensions={0} | all-to-all | bytes 2097152 | tf_op jit(solution)/shard_map/all_to_all | solution.py:57
  174.1 0.0 all-gather.5.cloned.1.call-update
  174.2 3.6 all-to-all-start.2
  177.7 4.7 %broadcast_add_fusion = f32[256,4096]{1,0:T(8,128)} fusion(f32[256,4096]{1,0:T(8,128)} %param.17), kind=kLoop, calls=%fused_computation.17 | loop fusion | flops 1048576 | bytes 8388608 | tf_op jit(solution)/shard_map/add | solution.py:64
  182.5 11.1 %all-to-all-done.2 = bf16[8,256,256]{2,1,0:T(8,128)(2,1)S(1)} async-done(((bf16[8,256,256]{2,1,0:T(8,128)(2,1)}), bf16[8,256,256]{2,1,0:T(8,128)(2,1)S(1)}, u32[]{:S(2)}, u32[]{:S(2)}) %all-to-all-start.2) | async-done | bytes 1048608 | tf_op jit(solution)/shard_map/all_to_all | solution.py:56
  193.6 0.2 bitcast_convert_fusion
  193.8 1.9 copy.25
  195.7 96.4 %all-gather.5.cloned.1.call-done = bf16[8,256,4096]{2,1,0:T(8,128)(2,1)} async-done(((bf16[8,256,256]{2,1,0:T(8,128)(2,1)}), bf16[8,256,4096]{2,1,0:T(8,128)(2,1)}) %all-gather.5.cloned.1.call-update) | async-done | bytes 16777232 | tf_op jit(solution)/shard_map/all_gather | solution.py:59
  292.1 46.7 %while.10 = (s32[]{:T(128)}, f32[4,16]{1,0:T(4,128)S(1)}, bf16[4,256,256]{2,1,0:T(8,128)(2,1)}, bf16[4,256,4096]{2,1,0:T(8,128)(2,1)}, f32[256,4096]{1,0:T(8,128...) while((s32[]{:T(128)}, f32[4,16]{1,0:T(4,128)S(1)}, ...), condition=%wide.region_6.8_spmd, body=%wide.region_3.7_spmd.sunk | while | flops 4834983936 | bytes 25314592 | solution.py:76
  292.1 11.5 %fusion.30 = f32[2048]{0:T(1024)S(1)} fusion(f32[2048,256]{0,1:T(8,128)} %get-tuple-element.133, bf16[2048,4096]{1,0:T(8,128)(2,1)} %get-tuple-element.132, f32[256,4096]{1,0:T(8,128)} %get-tuple-element.131, bf16[4,256,4096]{2,1,0:T(8,128)(2,1)} %get-tuple-element.130, s32[]{:T(128)} %get-tuple-element.118, bf16[4,256,256]{2,1,0:T(8,128)(2,1)} %get-tuple-element.129), kind=kOutput, calls=%fused_computation.8.clone.1 | convolution fusion | flops 4834981888 | bytes 25306112 | tf_op jit(solution)/shard_map/while/body/eval_jaxpr/dot_general | solution.py:70
  303.6 0.1 bitcast_reduce_fusion.2
  303.7 11.5 %fusion.30 = f32[2048]{0:T(1024)S(1)} fusion(f32[2048,256]{0,1:T(8,128)} %get-tuple-element.133, bf16[2048,4096]{1,0:T(8,128)(2,1)} %get-tuple-element.132, f32[256,4096]{1,0:T(8,128)} %get-tuple-element.131, bf16[4,256,4096]{2,1,0:T(8,128)(2,1)} %get-tuple-element.130, s32[]{:T(128)} %get-tuple-element.118, bf16[4,256,256]{2,1,0:T(8,128)(2,1)} %get-tuple-element.129), kind=kOutput, calls=%fused_computation.8.clone.1 | convolution fusion | flops 4834981888 | bytes 25306112 | tf_op jit(solution)/shard_map/while/body/eval_jaxpr/dot_general | solution.py:70
  315.2 0.1 bitcast_reduce_fusion.2
  315.4 11.5 %fusion.30 = f32[2048]{0:T(1024)S(1)} fusion(f32[2048,256]{0,1:T(8,128)} %get-tuple-element.133, bf16[2048,4096]{1,0:T(8,128)(2,1)} %get-tuple-element.132, f32[256,4096]{1,0:T(8,128)} %get-tuple-element.131, bf16[4,256,4096]{2,1,0:T(8,128)(2,1)} %get-tuple-element.130, s32[]{:T(128)} %get-tuple-element.118, bf16[4,256,256]{2,1,0:T(8,128)(2,1)} %get-tuple-element.129), kind=kOutput, calls=%fused_computation.8.clone.1 | convolution fusion | flops 4834981888 | bytes 25306112 | tf_op jit(solution)/shard_map/while/body/eval_jaxpr/dot_general | solution.py:70
  326.9 0.1 bitcast_reduce_fusion.2
  327.1 11.5 %fusion.30 = f32[2048]{0:T(1024)S(1)} fusion(f32[2048,256]{0,1:T(8,128)} %get-tuple-element.133, bf16[2048,4096]{1,0:T(8,128)(2,1)} %get-tuple-element.132, f32[256,4096]{1,0:T(8,128)} %get-tuple-element.131, bf16[4,256,4096]{2,1,0:T(8,128)(2,1)} %get-tuple-element.130, s32[]{:T(128)} %get-tuple-element.118, bf16[4,256,256]{2,1,0:T(8,128)(2,1)} %get-tuple-element.129), kind=kOutput, calls=%fused_computation.8.clone.1 | convolution fusion | flops 4834981888 | bytes 25306112 | tf_op jit(solution)/shard_map/while/body/eval_jaxpr/dot_general | solution.py:70
  338.6 0.1 bitcast_reduce_fusion.2
  338.7 38.2 %psum.7 = f32[4,16]{1,0:T(4,128)S(1)} all-reduce(f32[4,16]{1,0:T(4,128)S(1)} %get-tuple-element.43), channel_id=1, replica_groups=mesh['dp'=8,'eig'=16] {'eig'}, use_global_device_ids=true, to_apply=%region_7.9 | all-reduce | flops 64 | bytes 512 | tf_op jit(solution)/shard_map/psum | solution.py:77
  376.9 0.6 broadcast_multiply_fusion
  (9 shorter events, 0.2 us)
Async XLA Ops:
  6.5 116.9 %all-gather.3.cloned.1.call-start = ((), (), s32[]{:S(2)}) async-start(), calls=%async_computation.3 | async-start | bytes 17825792 | tf_op jit(solution)/shard_map/all_gather | solution.py:24
  11.4 9.7 %all-to-all-start = ((s32[1,8,2]{2,0,1:T(1,128)}), s32[1,8,2]{2,0,1:T(1,128)S(1)}, u32[]{:S(2)}, u32[]{:S(2)}) async-start(s32[1,8,2]{2,0,1:T(1,128)} %bitcast.6), calls=%async_computation | async-start | bytes 8192 | tf_op jit(solution)/shard_map/all_to_all | solution.py:33
  15.8 276.3 %all-gather.5.cloned.1.call-start = ((), (), s32[]{:S(2)}) async-start(), calls=%async_computation.4 | async-start | bytes 17825792 | tf_op jit(solution)/shard_map/all_gather | solution.py:59
  174.2 19.4 %all-to-all-start.2 = ((bf16[8,256,256]{2,1,0:T(8,128)(2,1)}), bf16[8,256,256]{2,1,0:T(8,128)(2,1)S(1)}, u32[]{:S(2)}, u32[]{:S(2)}) async-start(bf16[8,256,256]{2,1,0:T(8,128)(2,1)} %get-tuple-element.62), calls=%async_computation.2 | async-start | bytes 2097152 | tf_op jit(solution)/shard_map/all_to_all | solution.py:56
Sparse Core Ops, SparseCore 0:
  9.5 113.8 all-gather.2
  174.3 117.7 all-gather.4
where the time goes:
time: 385 us; the launch traced here: 384 us
  waiting for transfers between devices  212 us (55%)
  matrix products  59.9 us (16%)
  blocking collectives  58.3 us (15%)
  local copies, waits for them, and re-layouts  18.4 us (5%)
  other arithmetic  13.8 us (4%)
  between operations  13.5 us (4%)
  starting transfers between devices  8.02 us (2%)
    all_gather x1, waiting for transfers between devices, shards(): shard_rows = lax.all_gather(stacked, 'eig', axis=1, tiled=True)  101 us
    all_gather x1, waiting for transfers between devices, shards(): act_recv = lax.all_gather(act_narrow, 'eig', axis=2, tiled=True)  96.4 us
    dot_general x4, matrix products, score_query(): lax.dot_general(act_flat, precond, (((1,), (1,)), ((), ())), preferred_el...  46 us
    psum x1, blocking collectives, shards(): summed = lax.psum(partial_sums, 'eig')  38.2 us
    all_to_all x1, blocking collectives, shards(): lax.all_to_all(pack_rows(act_block), 'dp', split_axis=0, concat_axis=0, t...  20.1 us
    gather x2, local copies, waits for them, and re-layouts, pack_rows(): jnp.take(source, row_index, axis=0)  15 us
    all_to_all x1, waiting for transfers between devices, shards(): lax.all_to_all(grad_pack, 'dp', split_axis=0, concat_axis=0, tiled=True)  11.1 us
  transfers between devices with their start and end apart: 4, of which 4 were waited for; matrix products, arithmetic and copies ran while one was open for 3% of the time, Pallas kernels for 0%

commit v1 on v0

v1 whole, which is shorter than its diff:
```python
import math

import jax
import jax.numpy as jnp
from jax import lax
from jax.sharding import PartitionSpec as P

DAMPING = 0.1


def shards(
    acts,
    grads,
    act_basis,
    grad_basis,
    eigenvalues,
    query_grads,
    query_acts,
    cand_local,
    seq_lengths,
):
    block_width = act_basis.shape[0]
    queries = query_grads.shape[0]
    full_width = query_acts.shape[2]
    seq_count = seq_lengths.shape[1]
    group_rows = acts.shape[0] * lax.axis_size("eig")
    max_len = 2 * group_rows // seq_count

    pick_lists = lax.all_to_all(cand_local, "dp", split_axis=1, concat_axis=0, tiled=True)
    owners = pick_lists.shape[0]
    per_shard = pick_lists.shape[1]
    lengths = seq_lengths[0]
    offsets = jnp.cumsum(lengths) - lengths
    chosen = (
        pick_lists[:, :, None] == jnp.arange(seq_count, dtype=jnp.int32)[None, None, :]
    ).astype(jnp.int32)
    pick_len = jnp.sum(chosen * lengths[None, None, :], axis=2)
    pick_start = jnp.sum(chosen * offsets[None, None, :], axis=2)
    within = jnp.arange(max_len, dtype=jnp.int32)
    is_live = within[None, None, :] < pick_len[:, :, None]
    row_index = jnp.where(is_live, pick_start[:, :, None] + within[None, None, :], -1).reshape(-1)
    select = (row_index[:, None] == jnp.arange(group_rows, dtype=jnp.int32)[None, :]).astype(
        jnp.bfloat16
    )

    def rotate_and_pack(rows, basis):
        shard_rows = lax.all_gather(rows, "eig", axis=0, tiled=True)
        rotated = jnp.dot(shard_rows, basis.T, preferred_element_type=jnp.float32).astype(
            jnp.bfloat16
        )
        rotated = lax.optimization_barrier(rotated)
        packed = jnp.dot(select, rotated, preferred_element_type=jnp.float32).astype(jnp.bfloat16)
        packed = packed.reshape(owners, per_shard * max_len, block_width)
        return lax.all_to_all(packed, "dp", split_axis=0, concat_axis=0, tiled=True)

    act_narrow = rotate_and_pack(acts, act_basis)
    act_recv = lax.all_gather(act_narrow, "eig", axis=2, tiled=True)
    grad_recv = rotate_and_pack(grads, grad_basis)

    slot_count = owners * per_shard * max_len
    grad_flat = grad_recv.reshape(slot_count, block_width).astype(jnp.float32)
    act_flat = act_recv.reshape(slot_count, full_width)

    damped = eigenvalues + DAMPING
    query_outer = jnp.einsum(
        "qti,qtk->qik", query_grads, query_acts, preferred_element_type=jnp.float32
    )
    precond = (query_outer / damped[None]).astype(jnp.bfloat16)
    precond = lax.optimization_barrier(precond.reshape(queries * block_width, full_width))
    projected = lax.dot_general(
        act_flat, precond, (((1,), (1,)), ((), ())), preferred_element_type=jnp.float32
    )
    projected = lax.optimization_barrier(projected).reshape(slot_count, queries, block_width)
    per_token = jnp.sum(projected * grad_flat[:, None, :], axis=2)
    partial_sums = jnp.sum(per_token.reshape(owners * per_shard, max_len, queries), axis=1).T

    summed = lax.psum(partial_sums, "eig")
    score_scale = 1.0 / (full_width * 4.0 * math.sqrt(query_acts.shape[1]))
    return summed * score_scale


def solution(mesh):
    placed = (
        P(("dp", "eig"), None),
        P(("dp", "eig"), None),
        P("eig", None),
        P("eig", None),
        P("eig", None),
        P("dp", None, "eig"),
        P("dp", None, None),
        P("dp", None),
        P("dp", None),
    )
    return jax.shard_map(
        shards, mesh=mesh, in_specs=placed, out_specs=P("dp", None), check_vma=False
    )
```

time: 385 us -> 364 us (0.945)
  matrix products: 59.9 us -> 50.1 us
  waiting for transfers between devices: 212 us -> 203 us
  local copies, waits for them, and re-layouts: 18.4 us -> 13.2 us
    gather x2 -> x0, local copies, waits for them, and re-layouts: 15 us -> none  [pack_rows(): jnp.take(source, row_index, axis=0)]
    reshape x0 -> x1, local copies, waits for them, and re-layouts: none -> 10.6 us  [shards(): lax.optimization_barrier(projected)]
    dot_general x6, matrix products: 59.9 us -> 50.1 us  [the longest x1 24.1 us: shards(): lax.dot_general(act_flat, precond, (((1,), (1,)), ((), ())), preferred_el...]
    all_gather x1, waiting for transfers between devices: 96.4 us -> 90.2 us  [shards(): act_recv = lax.all_gather(act_narrow, 'eig', axis=2, tiled=True)]
    reduce_sum x4 -> x2, other arithmetic: 0.44 us -> 6.38 us  [the longest x1 6.29 us: shards(): per_token = jnp.sum(projected * grad_flat[:, None, :], axis=2)]
    all_to_all x1, waiting for transfers between devices: 11.1 us -> 6.71 us  [rotate_and_pack(): return lax.all_to_all(packed, 'dp', split_axis=0, concat_axis=0, tiled=True)]
    all_gather x1 -> x2, waiting for transfers between devices: 101 us -> 101 us  [rotate_and_pack(): shard_rows = lax.all_gather(rows, 'eig', axis=0, tiled=True)]
  transfers between devices with their start and end apart: 4 -> 5, of which waited for: 4 -> 5; matrix products, arithmetic and copies ran while one was open for 3% -> 10% of each run, Pallas kernels for 0% -> 0%
where the time goes in v1:
time: 364 us
  waiting for transfers between devices  203 us (56%)
  blocking collectives  58.3 us (16%)
  matrix products  50.1 us (14%)
  other arithmetic  16.9 us (5%)
  local copies, waits for them, and re-layouts  13.2 us (4%)
  between operations  13.2 us (4%)
  starting transfers between devices  8.75 us (2%)
    all_gather x2, waiting for transfers between devices, rotate_and_pack(): shard_rows = lax.all_gather(rows, 'eig', axis=0, tiled=True)  101 us
    all_gather x1, waiting for transfers between devices, shards(): act_recv = lax.all_gather(act_narrow, 'eig', axis=2, tiled=True)  90.2 us
    psum x1, blocking collectives, shards(): summed = lax.psum(partial_sums, 'eig')  38.1 us
    dot_general x1, matrix products, shards(): lax.dot_general(act_flat, precond, (((1,), (1,)), ((), ())), preferred_el...  24.1 us
    all_to_all x1, blocking collectives, rotate_and_pack(): return lax.all_to_all(packed, 'dp', split_axis=0, concat_axis=0, tiled=True)  20.1 us
    dot_general x2, matrix products, rotate_and_pack(): jnp.dot(shard_rows, basis.T, preferred_element_type=jnp.float32)  13.9 us
    reshape x1, local copies, waits for them, and re-layouts, shards(): lax.optimization_barrier(projected)  10.6 us
    dot_general x1, matrix products, shards(): jnp.einsum('qti,qtk->qik', query_grads, query_acts, preferred_element_typ...  9.21 us
  transfers between devices with their start and end apart: 5, of which 5 were waited for; matrix products, arithmetic and copies ran while one was open for 10% of the time, Pallas kernels for 0%

profile of v1, /device:TPU:0, one launch (start us, length us, event | category | flops | bytes accessed | tf_op | source)
XLA Modules:
  0.0 363.8 jit_solution(16105542730583716110)
XLA Ops:
  6.5 0.0 copy-start
  6.5 0.0 all-gather.4.cloned.1.call-start
  6.5 0.7 all-gather.4.cloned.1.call-update
  7.3 0.0 all-gather.8.cloned.1.call-start
  7.3 0.7 all-gather.8.cloned.1.call-update
  8.0 0.5 broadcast.27
  8.5 1.3 reduce.3
  9.8 0.7 all_to_all.16
  10.5 4.4 %all-to-all-start = ((s32[1,8,2]{2,0,1:T(1,128)}), s32[1,8,2]{2,0,1:T(1,128)S(1)}, u32[]{:S(2)}, u32[]{:S(2)}) async-start(s32[1,8,2]{2,0,1:T(1,128)} %bitcast), calls=%async_computation | async-start | bytes 8192 | tf_op jit(solution)/shard_map/all_to_all | solution.py:29
  14.9 0.0 all-gather.6.cloned.1.call-start
  15.0 0.8 reduce-window.8
  15.8 0.7 bitcast_subtract_fusion
  16.5 3.7 %all-to-all-done = s32[1,8,2]{2,0,1:T(1,128)S(1)} async-done(((s32[1,8,2]{2,0,1:T(1,128)}), s32[1,8,2]{2,0,1:T(1,128)S(1)}, u32[]{:S(2)}, u32[]{:S(2)}) %all-to-all-start) | async-done | bytes 96 | tf_op jit(solution)/shard_map/all_to_all | solution.py:29
  20.2 0.1 copy.26
  20.3 0.9 select_reduce_fusion.1
  21.2 0.1 copy.27
  21.2 0.1 copy.28
  21.3 0.1 compare_select_fusion
  21.4 61.6 %all-gather.4.cloned.1.call-done = bf16[512,8192]{1,0:T(8,128)(2,1)} async-done(((bf16[32,8192]{1,0:T(8,128)(2,1)}), bf16[512,8192]{1,0:T(8,128)(2,1)}) %all-gather.4.cloned.1.call-update) | async-done | bytes 8388624 | tf_op jit(solution)/shard_map/all_gather | solution.py:47
  83.0 6.9 %convolution_convert_fusion.1 = bf16[512,256]{1,0:T(8,128)(2,1)S(1)} fusion(bf16[512,8192]{1,0:T(8,128)(2,1)} %all-gather.4.cloned.1.call-done, bf16[256,8192]{1,0:T(8,128)(2,1)} %param.11), kind=kOutput, calls=%fused_computation.11 | convolution fusion | flops 2147614720 | bytes 12845056 | tf_op jit(solution)/shard_map/dot_general | solution.py:48
  89.9 1.1 fusion.2
  91.0 20.1 %all_to_all.23 = bf16[8,256,256]{2,1,0:T(8,128)(2,1)} all-to-all(bf16[8,256,256]{2,1,0:T(8,128)(2,1)S(1)} %bitcast.28), channel_id=1, replica_groups=mesh['dp'=8,'eig'=16] {'dp'}, dimensions={0} | all-to-all | bytes 2097152 | tf_op jit(solution)/shard_map/all_to_all | solution.py:54
  111.1 0.0 all-gather.6.cloned.1.call-update
  111.2 4.8 %broadcast_add_fusion = f32[256,4096]{1,0:T(8,128)} fusion(f32[256,4096]{1,0:T(8,128)} %param.13), kind=kLoop, calls=%fused_computation.7 | loop fusion | flops 1048576 | bytes 8388608 | tf_op jit(solution)/shard_map/add | solution.py:64
  115.9 39.8 %all-gather.8.cloned.1.call-done = bf16[512,8192]{1,0:T(8,128)(2,1)} async-done(((bf16[32,8192]{1,0:T(8,128)(2,1)}), bf16[512,8192]{1,0:T(8,128)(2,1)}) %all-gather.8.cloned.1.call-update) | async-done | bytes 8388624 | tf_op jit(solution)/shard_map/all_gather | solution.py:47
  155.7 6.9 %convolution_convert_fusion = bf16[512,256]{1,0:T(8,128)(2,1)S(1)} fusion(bf16[512,8192]{1,0:T(8,128)(2,1)} %all-gather.8.cloned.1.call-done, bf16[256,8192]{1,0:T(8,128)(2,1)} %param.12), kind=kOutput, calls=%fused_computation.10 | convolution fusion | flops 2147614720 | bytes 12845056 | tf_op jit(solution)/shard_map/dot_general | solution.py:48
  162.6 1.9 fusion.3
  164.5 4.3 %all-to-all-start.2 = ((bf16[8,256,256]{2,1,0:T(8,128)(2,1)}), bf16[8,256,256]{2,1,0:T(8,128)(2,1)S(1)}, u32[]{:S(2)}, u32[]{:S(2)}) async-start(bf16[8,256,256]{2,1,0:T(8,128)(2,1)} %bitcast.9), calls=%async_computation.2 | async-start | bytes 2097152 | tf_op jit(solution)/shard_map/all_to_all | solution.py:54
  168.7 0.0 copy-done
  168.7 9.2 %divide_convert_fusion = bf16[4,256,4096]{2,1,0:T(8,128)(2,1)} fusion(f32[256,4096]{1,0:T(8,128)} %broadcast_add_fusion, bf16[4,256,256]{2,1,0:T(8,128)(2,1)S(1)} %copy-done, bf16[4,256,4096]{2,1,0:T(8,128)(2,1)} %param.15), kind=kOutput, calls=%fused_computation | convolution fusion | flops 2155872256 | bytes 21495808 | tf_op jit(solution)/shard_map/qti,qtk->qik/dot_general | solution.py:65
  177.9 6.7 %all-to-all-done.2 = bf16[8,256,256]{2,1,0:T(8,128)(2,1)S(1)} async-done(((bf16[8,256,256]{2,1,0:T(8,128)(2,1)}), bf16[8,256,256]{2,1,0:T(8,128)(2,1)S(1)}, u32[]{:S(2)}, u32[]{:S(2)}) %all-to-all-start.2) | async-done | bytes 1048608 | tf_op jit(solution)/shard_map/all_to_all | solution.py:54
  184.7 0.0 copy-start.2
  184.7 1.1 copy-done.2
  185.7 1.4 convert.1
  187.1 90.2 %all-gather.6.cloned.1.call-done = bf16[8,256,4096]{2,1,0:T(8,128)(2,1)} async-done(((bf16[8,256,256]{2,1,0:T(8,128)(2,1)}), bf16[8,256,4096]{2,1,0:T(8,128)(2,1)}) %all-gather.6.cloned.1.call-update) | async-done | bytes 16777232 | tf_op jit(solution)/shard_map/all_gather | solution.py:57
  277.4 24.1 %fusion.6 = f32[2048,1024]{1,0:T(8,128)} fusion(bf16[2048,4096]{1,0:T(8,128)(2,1)} %bitcast.35, bf16[1024,4096]{1,0:T(8,128)(2,1)} %bitcast.36), kind=kOutput, calls=%fused_computation.19 | convolution fusion | flops 17179869184 | bytes 33554432 | tf_op jit(solution)/shard_map/dot_general | solution.py:70
  301.5 0.0 copy-start.1
  301.5 10.6 %reshape.106 = f32[2048,4,256]{2,1,0:T(4,128)} reshape(f32[2048,1024]{1,0:T(8,128)} %fusion.6) | data formatting | bytes 16777216 | tf_op jit(solution)/shard_map/reshape | solution.py:73
  312.1 6.3 %multiply_reduce_fusion = f32[2048,4]{1,0:T(8,128)S(1)} fusion(f32[2048,4,256]{2,1,0:T(4,128)} %reshape.106, f32[2048,256]{1,0:T(8,128)S(1)} %convert.1), kind=kLoop, calls=%fused_computation.1 | loop fusion | flops 4186112 | bytes 10518528 | tf_op jit(solution)/shard_map/reduce_sum | solution.py:74
  318.4 0.1 bitcast_reduce_fusion
  318.5 0.1 copy.32
  318.6 38.1 %psum.7 = f32[4,16]{1,0:T(4,128)S(1)} all-reduce(f32[4,16]{1,0:T(4,128)S(1)} %bitcast.29), channel_id=1, replica_groups=mesh['dp'=8,'eig'=16] {'eig'}, use_global_device_ids=true, to_apply=%region_5.6 | all-reduce | flops 64 | bytes 512 | tf_op jit(solution)/shard_map/psum | solution.py:77
  356.7 0.6 broadcast_multiply_fusion
  357.3 0.0 copy-done.1
Async XLA Ops:
  6.5 162.2 %copy-start = (bf16[4,256,256]{2,1,0:T(8,128)(2,1)S(1)}, bf16[4,256,256]{2,1,0:T(8,128)(2,1)}, u32[]{:S(2)}) copy-start(bf16[4,256,256]{2,1,0:T(8,128)(2,1)} %param.14) | copy-start | bytes 1572868
  6.5 76.4 %all-gather.4.cloned.1.call-start = ((), (), s32[]{:S(2)}) async-start(), calls=%async_computation.3 | async-start | bytes 8912896 | tf_op jit(solution)/shard_map/all_gather | solution.py:47
  7.3 148.4 %all-gather.8.cloned.1.call-start = ((), (), s32[]{:S(2)}) async-start(), calls=%async_computation.5 | async-start | bytes 8912896 | tf_op jit(solution)/shard_map/all_gather | solution.py:47
  10.5 9.7 %all-to-all-start = ((s32[1,8,2]{2,0,1:T(1,128)}), s32[1,8,2]{2,0,1:T(1,128)S(1)}, u32[]{:S(2)}, u32[]{:S(2)}) async-start(s32[1,8,2]{2,0,1:T(1,128)} %bitcast), calls=%async_computation | async-start | bytes 8192 | tf_op jit(solution)/shard_map/all_to_all | solution.py:29
  14.9 262.5 %all-gather.6.cloned.1.call-start = ((), (), s32[]{:S(2)}) async-start(), calls=%async_computation.4 | async-start | bytes 17825792 | tf_op jit(solution)/shard_map/all_gather | solution.py:57
  164.5 20.2 %all-to-all-start.2 = ((bf16[8,256,256]{2,1,0:T(8,128)(2,1)}), bf16[8,256,256]{2,1,0:T(8,128)(2,1)S(1)}, u32[]{:S(2)}, u32[]{:S(2)}) async-start(bf16[8,256,256]{2,1,0:T(8,128)(2,1)} %bitcast.9), calls=%async_computation.2 | async-start | bytes 2097152 | tf_op jit(solution)/shard_map/all_to_all | solution.py:54
  184.7 1.1 copy-start.2
  301.5 55.8 %copy-start.1 = (bf16[4,256,256]{2,1,0:T(8,128)(2,1)S(1)}, bf16[4,256,256]{2,1,0:T(8,128)(2,1)}, u32[]{:S(2)}) copy-start(bf16[4,256,256]{2,1,0:T(8,128)(2,1)} %param.14) | copy-start | bytes 1572868
Sparse Core Ops, SparseCore 0:
  9.5 73.4 all-gather.3
  85.1 70.4 all-gather.7
  157.8 119.5 all-gather.5

commit v2 on v1

--- a/solution.py
+++ b/solution.py
@@ -1,11 +1,51 @@
 import math
+
+import functools
 
 import jax
 import jax.numpy as jnp
 from jax import lax
+from jax.experimental import pallas as pl
 from jax.sharding import PartitionSpec as P
 
 DAMPING = 0.1
+
+
+def _score_body(queries, width, a_ref, p_ref, g_ref, o_ref):
+    a = a_ref[...]
+    g = g_ref[...].astype(jnp.float32)
+    cols = []
+    for q in range(queries):
+        proj = lax.dot_general(
+            a,
+            p_ref[q * width : (q + 1) * width, :],
+            (((1,), (1,)), ((), ())),
+            preferred_element_type=jnp.float32,
+        )
+        cols.append(jnp.sum(proj * g, axis=1, keepdims=True))
+    o_ref[...] = jnp.concatenate(cols, axis=1)
+
+
+def score_rows(act_flat, precond, grad_flat, queries, tile=256):
+    rows, full = act_flat.shape
+    width = grad_flat.shape[1]
+    return pl.pallas_call(
+        functools.partial(_score_body, queries, width),
+        grid=(rows // tile,),
+        in_specs=[
+            pl.BlockSpec((tile, full), lambda i: (i, 0)),
+            pl.BlockSpec((queries * width, full), lambda i: (0, 0)),
+            pl.BlockSpec((tile, width), lambda i: (i, 0)),
+        ],
+        out_specs=pl.BlockSpec((tile, queries), lambda i: (i, 0)),
+        out_shape=jax.ShapeDtypeStruct((rows, queries), jnp.float32),
+        cost_estimate=pl.CostEstimate(
+            flops=2 * rows * full * queries * width,
+            transcendentals=0,
+            bytes_accessed=2 * (rows * full + queries * width * full + rows * width)
+            + 4 * rows * queries,
+        ),
+    )(act_flat, precond, grad_flat)
 
 
 def shards(
@@ -58,7 +98,7 @@
     grad_recv = rotate_and_pack(grads, grad_basis)
 
     slot_count = owners * per_shard * max_len
-    grad_flat = grad_recv.reshape(slot_count, block_width).astype(jnp.float32)
+    grad_flat = grad_recv.reshape(slot_count, block_width)
     act_flat = act_recv.reshape(slot_count, full_width)
 
     damped = eigenvalues + DAMPING
@@ -67,14 +107,16 @@
     )
     precond = (query_outer / damped[None]).astype(jnp.bfloat16)
     precond = lax.optimization_barrier(precond.reshape(queries * block_width, full_width))
-    projected = lax.dot_general(
-        act_flat, precond, (((1,), (1,)), ((), ())), preferred_element_type=jnp.float32
-    )
-    projected = lax.optimization_barrier(projected).reshape(slot_count, queries, block_width)
-    per_token = jnp.sum(projected * grad_flat[:, None, :], axis=2)
+    per_token = score_rows(act_flat, precond, grad_flat, queries)
     partial_sums = jnp.sum(per_token.reshape(owners * per_shard, max_len, queries), axis=1).T
 
-    summed = lax.psum(partial_sums, "eig")
+    summed = partial_sums
+    group = lax.axis_size("eig")
+    stride = 1
+    while stride < group:
+        pairs = [(i, i ^ stride) for i in range(group)]
+        summed = summed + lax.ppermute(summed, "eig", pairs)
+        stride *= 2
     score_scale = 1.0 / (full_width * 4.0 * math.sqrt(query_acts.shape[1]))
     return summed * score_scale
 

time: 364 us -> 329 us (0.904)
  blocking collectives: 58.3 us -> 20.1 us
  Pallas kernels: 0 us -> 25.1 us
  matrix products: 50.1 us -> 26.1 us
  waiting for transfers between devices: 203 us -> 217 us
  local copies, waits for them, and re-layouts: 13.2 us -> 2.1 us
  other arithmetic: 16.9 us -> 9.83 us
  starting transfers between devices: 8.75 us -> 14.9 us
    psum x1 -> x0, blocking collectives: 38.1 us -> none  [shards(): summed = lax.psum(partial_sums, 'eig')]
    pallas_call x0 -> x1, Pallas kernels: none -> 25.1 us  [score_rows(): pl.pallas_call(functools.partial(_score_body, queries, width), grid=(rows...]
    dot_general x1 -> x0, matrix products: 24.1 us -> none  [shards(): lax.dot_general(act_flat, precond, (((1,), (1,)), ((), ())), preferred_el...]
    ppermute x0 -> x4, waiting for transfers between devices: none -> 11.5 us  [shards(): summed = summed + lax.ppermute(summed, 'eig', pairs)]
    reshape x1 -> x0, local copies, waits for them, and re-layouts: 10.6 us -> none  [shards(): lax.optimization_barrier(projected)]
    reduce_sum x1 -> x0, other arithmetic: 6.29 us -> none  [shards(): per_token = jnp.sum(projected * grad_flat[:, None, :], axis=2)]
    ppermute x0 -> x4, starting transfers between devices: none -> 6.15 us  [shards(): summed = summed + lax.ppermute(summed, 'eig', pairs)]
  transfers between devices with their start and end apart: 5 -> 9, of which waited for: 5 -> 9; matrix products, arithmetic and copies ran while one was open for 10% -> 11% of each run, Pallas kernels for 0% -> 0%
where the time goes in v2:
time: 329 us
  waiting for transfers between devices  217 us (66%)
  matrix products  26.1 us (8%)
  Pallas kernels  25.1 us (8%)
  blocking collectives  20.1 us (6%)
  starting transfers between devices  14.9 us (5%)
  between operations  13.2 us (4%)
  other arithmetic  9.83 us (3%)
    all_gather x2, waiting for transfers between devices, rotate_and_pack(): shard_rows = lax.all_gather(rows, 'eig', axis=0, tiled=True)  101 us
    all_gather x1, waiting for transfers between devices, shards(): act_recv = lax.all_gather(act_narrow, 'eig', axis=2, tiled=True)  92.7 us
    pallas_call x1, Pallas kernels, score_rows(): pl.pallas_call(functools.partial(_score_body, queries, width), grid=(rows...  25.1 us
    all_to_all x1, blocking collectives, rotate_and_pack(): return lax.all_to_all(packed, 'dp', split_axis=0, concat_axis=0, tiled=True)  20.1 us
    dot_general x2, matrix products, rotate_and_pack(): jnp.dot(shard_rows, basis.T, preferred_element_type=jnp.float32)  13.9 us
    ppermute x4, waiting for transfers between devices, shards(): summed = summed + lax.ppermute(summed, 'eig', pairs)  11.5 us
    dot_general x1, matrix products, shards(): jnp.einsum('qti,qtk->qik', query_grads, query_acts, preferred_element_typ...  9.26 us
    all_to_all x1, waiting for transfers between devices, rotate_and_pack(): return lax.all_to_all(packed, 'dp', split_axis=0, concat_axis=0, tiled=True)  6.66 us
  transfers between devices with their start and end apart: 9, of which 9 were waited for; matrix products, arithmetic and copies ran while one was open for 11% of the time, Pallas kernels for 0%

profile of v2, /device:TPU:0, one launch (start us, length us, event | category | flops | bytes accessed | tf_op | source)
XLA Modules:
  0.0 328.7 jit_solution(12019471614810903068)
XLA Ops:
  6.5 0.0 copy-start
  6.5 0.0 all-gather.4.cloned.1.call-start
  6.5 0.7 all-gather.4.cloned.1.call-update
  7.3 0.0 all-gather.8.cloned.1.call-start
  7.3 0.7 all-gather.8.cloned.1.call-update
  8.0 0.5 broadcast.27
  8.5 1.3 reduce.3
  9.8 0.7 all_to_all.16
  10.5 4.4 %all-to-all-start = ((s32[1,8,2]{2,0,1:T(1,128)}), s32[1,8,2]{2,0,1:T(1,128)S(1)}, u32[]{:S(2)}, u32[]{:S(2)}) async-start(s32[1,8,2]{2,0,1:T(1,128)} %bitcast), calls=%async_computation | async-start | bytes 8192 | tf_op jit(solution)/shard_map/all_to_all | solution.py:69
  14.9 0.0 all-gather.6.cloned.1.call-start
  15.0 0.8 reduce-window.8
  15.8 0.7 bitcast_subtract_fusion
  16.5 3.8 %all-to-all-done = s32[1,8,2]{2,0,1:T(1,128)S(1)} async-done(((s32[1,8,2]{2,0,1:T(1,128)}), s32[1,8,2]{2,0,1:T(1,128)S(1)}, u32[]{:S(2)}, u32[]{:S(2)}) %all-to-all-start) | async-done | bytes 96 | tf_op jit(solution)/shard_map/all_to_all | solution.py:69
  20.2 0.1 copy.22
  20.3 0.9 select_reduce_fusion.1
  21.2 0.1 copy.23
  21.2 0.1 copy.24
  21.3 0.1 compare_select_fusion
  21.4 61.6 %all-gather.4.cloned.1.call-done = bf16[512,8192]{1,0:T(8,128)(2,1)} async-done(((bf16[32,8192]{1,0:T(8,128)(2,1)}), bf16[512,8192]{1,0:T(8,128)(2,1)}) %all-gather.4.cloned.1.call-update) | async-done | bytes 8388624 | tf_op jit(solution)/shard_map/all_gather | solution.py:87
  83.0 6.9 %convolution_convert_fusion.1 = bf16[512,256]{1,0:T(8,128)(2,1)S(1)} fusion(bf16[512,8192]{1,0:T(8,128)(2,1)} %all-gather.4.cloned.1.call-done, bf16[256,8192]{1,0:T(8,128)(2,1)} %param.11), kind=kOutput, calls=%fused_computation.10 | convolution fusion | flops 2147614720 | bytes 12845056 | tf_op jit(solution)/shard_map/dot_general | solution.py:88
  89.9 1.1 fusion.2
  91.0 20.1 %all_to_all.23 = bf16[8,256,256]{2,1,0:T(8,128)(2,1)} all-to-all(bf16[8,256,256]{2,1,0:T(8,128)(2,1)S(1)} %bitcast.26), channel_id=1, replica_groups=mesh['dp'=8,'eig'=16] {'dp'}, dimensions={0} | all-to-all | bytes 2097152 | tf_op jit(solution)/shard_map/all_to_all | solution.py:94
  111.1 0.0 all-gather.6.cloned.1.call-update
  111.2 4.7 %broadcast_add_fusion = f32[256,4096]{1,0:T(8,128)} fusion(f32[256,4096]{1,0:T(8,128)} %param.13), kind=kLoop, calls=%fused_computation.6 | loop fusion | flops 1048576 | bytes 8388608 | tf_op jit(solution)/shard_map/add | solution.py:104
  115.9 39.8 %all-gather.8.cloned.1.call-done = bf16[512,8192]{1,0:T(8,128)(2,1)} async-done(((bf16[32,8192]{1,0:T(8,128)(2,1)}), bf16[512,8192]{1,0:T(8,128)(2,1)}) %all-gather.8.cloned.1.call-update) | async-done | bytes 8388624 | tf_op jit(solution)/shard_map/all_gather | solution.py:87
  155.7 6.9 %convolution_convert_fusion = bf16[512,256]{1,0:T(8,128)(2,1)S(1)} fusion(bf16[512,8192]{1,0:T(8,128)(2,1)} %all-gather.8.cloned.1.call-done, bf16[256,8192]{1,0:T(8,128)(2,1)} %param.12), kind=kOutput, calls=%fused_computation.9 | convolution fusion | flops 2147614720 | bytes 12845056 | tf_op jit(solution)/shard_map/dot_general | solution.py:88
  162.6 1.9 fusion.3
  164.5 4.3 %all-to-all-start.2 = ((bf16[8,256,256]{2,1,0:T(8,128)(2,1)}), bf16[8,256,256]{2,1,0:T(8,128)(2,1)S(1)}, u32[]{:S(2)}, u32[]{:S(2)}) async-start(bf16[8,256,256]{2,1,0:T(8,128)(2,1)} %bitcast.9), calls=%async_computation.2 | async-start | bytes 2097152 | tf_op jit(solution)/shard_map/all_to_all | solution.py:94
  168.7 0.0 copy-done
  168.7 9.3 %divide_convert_fusion = bf16[4,256,4096]{2,1,0:T(8,128)(2,1)} fusion(f32[256,4096]{1,0:T(8,128)} %broadcast_add_fusion, bf16[4,256,256]{2,1,0:T(8,128)(2,1)S(1)} %copy-done, bf16[4,256,4096]{2,1,0:T(8,128)(2,1)} %param.15), kind=kOutput, calls=%fused_computation | convolution fusion | flops 2155872256 | bytes 21495808 | tf_op jit(solution)/shard_map/qti,qtk->qik/dot_general | solution.py:105
  178.0 6.7 %all-to-all-done.2 = bf16[8,256,256]{2,1,0:T(8,128)(2,1)S(1)} async-done(((bf16[8,256,256]{2,1,0:T(8,128)(2,1)}), bf16[8,256,256]{2,1,0:T(8,128)(2,1)S(1)}, u32[]{:S(2)}, u32[]{:S(2)}) %all-to-all-start.2) | async-done | bytes 1048608 | tf_op jit(solution)/shard_map/all_to_all | solution.py:94
  184.7 0.0 copy-start.2
  184.7 92.7 %all-gather.6.cloned.1.call-done = bf16[8,256,4096]{2,1,0:T(8,128)(2,1)} async-done(((bf16[8,256,256]{2,1,0:T(8,128)(2,1)}), bf16[8,256,4096]{2,1,0:T(8,128)(2,1)}) %all-gather.6.cloned.1.call-update) | async-done | bytes 16777232 | tf_op jit(solution)/shard_map/all_gather | solution.py:97
  277.4 0.0 copy-done.2
  277.4 0.0 copy-start.1
  277.4 25.1 %shard_map.91 = f32[2048,4]{1,0:T(8,128)} custom-call(bf16[2048,4096]{1,0:T(8,128)(2,1)} %bitcast.33, bf16[1024,4096]{1,0:T(8,128)(2,1)} %bitcast.34, bf16[2048,256]{1,0:T(8,128)(2,1)} %bitcast.25), custom_call_target="tpu_custom_call" | custom-call | flops 17179869184 | bytes 26247168 | tf_op jit(solution)/shard_map/pallas_call | solution.py:32
  302.5 1.3 bitcast_reduce_fusion
  303.8 1.3 collective-permute-start
  305.1 2.5 collective-permute-done
  307.5 1.8 collective-permute-start.1
  309.4 3.3 %collective-permute-done.1 = f32[4,16]{0,1:T(8,128)S(1)} collective-permute-done((f32[4,16]{0,1:T(8,128)S(1)}, f32[4,16]{0,1:T(8,128)S(1)}, u32[]{:S(2)}, u32[]{:S(2)}) %collective-permute-start.1) | collective-permute-done | bytes 288 | tf_op jit(solution)/shard_map/ppermute | solution.py:118
  312.7 1.2 collective-permute-start.2
  313.9 2.5 collective-permute-done.2
  316.3 1.9 collective-permute-start.3
  318.2 3.3 %collective-permute-done.3 = f32[4,16]{0,1:T(8,128)S(1)} collective-permute-done((f32[4,16]{0,1:T(8,128)S(1)}, f32[4,16]{0,1:T(8,128)S(1)}, u32[]{:S(2)}, u32[]{:S(2)}) %collective-permute-start.3) | collective-permute-done | bytes 288 | tf_op jit(solution)/shard_map/ppermute | solution.py:118
  321.5 0.7 copy.26
  322.2 0.0 copy-done.1
  (4 shorter events, 0.0 us)
Async XLA Ops:
  6.5 162.2 %copy-start = (bf16[4,256,256]{2,1,0:T(8,128)(2,1)S(1)}, bf16[4,256,256]{2,1,0:T(8,128)(2,1)}, u32[]{:S(2)}) copy-start(bf16[4,256,256]{2,1,0:T(8,128)(2,1)} %param.14) | copy-start | bytes 1572868
  6.5 76.4 %all-gather.4.cloned.1.call-start = ((), (), s32[]{:S(2)}) async-start(), calls=%async_computation.3 | async-start | bytes 8912896 | tf_op jit(solution)/shard_map/all_gather | solution.py:87
  7.3 148.4 %all-gather.8.cloned.1.call-start = ((), (), s32[]{:S(2)}) async-start(), calls=%async_computation.5 | async-start | bytes 8912896 | tf_op jit(solution)/shard_map/all_gather | solution.py:87
  10.5 9.7 %all-to-all-start = ((s32[1,8,2]{2,0,1:T(1,128)}), s32[1,8,2]{2,0,1:T(1,128)S(1)}, u32[]{:S(2)}, u32[]{:S(2)}) async-start(s32[1,8,2]{2,0,1:T(1,128)} %bitcast), calls=%async_computation | async-start | bytes 8192 | tf_op jit(solution)/shard_map/all_to_all | solution.py:69
  14.9 262.5 %all-gather.6.cloned.1.call-start = ((), (), s32[]{:S(2)}) async-start(), calls=%async_computation.4 | async-start | bytes 17825792 | tf_op jit(solution)/shard_map/all_gather | solution.py:97
  164.5 20.2 %all-to-all-start.2 = ((bf16[8,256,256]{2,1,0:T(8,128)(2,1)}), bf16[8,256,256]{2,1,0:T(8,128)(2,1)S(1)}, u32[]{:S(2)}, u32[]{:S(2)}) async-start(bf16[8,256,256]{2,1,0:T(8,128)(2,1)} %bitcast.9), calls=%async_computation.2 | async-start | bytes 2097152 | tf_op jit(solution)/shard_map/all_to_all | solution.py:94
  184.7 92.7 %copy-start.2 = (bf16[8,256,256]{2,1,0:T(8,128)(2,1)}, bf16[8,256,256]{2,1,0:T(8,128)(2,1)S(1)}, u32[]{:S(2)}) copy-start(bf16[8,256,256]{2,1,0:T(8,128)(2,1)S(1)} %all-to-all-done.2) | copy-start | bytes 3145732
  277.4 44.8 %copy-start.1 = (bf16[4,256,256]{2,1,0:T(8,128)(2,1)S(1)}, bf16[4,256,256]{2,1,0:T(8,128)(2,1)}, u32[]{:S(2)}) copy-start(bf16[4,256,256]{2,1,0:T(8,128)(2,1)} %param.14) | copy-start | bytes 1572868
  303.8 3.7 %collective-permute-start = (f32[4,16]{0,1:T(8,128)S(1)}, f32[4,16]{0,1:T(8,128)S(1)}, u32[]{:S(2)}, u32[]{:S(2)}) collective-permute-start(f32[4,16]{0,1:T(8,128)S(1)} %bitcast.27), channel_id=1, source_target_pairs={{0,1},{1,0},{2,3},{3,2},{4,5},{5,4},{6,7},{7,6},{8,9},{9,8},{10,11... | collective-permute-start | bytes 776 | tf_op jit(solution)/shard_map/ppermute | solution.py:118
  307.5 5.2 %collective-permute-start.1 = (f32[4,16]{0,1:T(8,128)S(1)}, f32[4,16]{0,1:T(8,128)S(1)}, u32[]{:S(2)}, u32[]{:S(2)}) collective-permute-start(f32[4,16]{0,1:T(8,128)S(1)} %bitcast_add_fusion), channel_id=1, source_target_pairs={{0,2},{1,3},{2,0},{3,1},{4,6},{5,7},{6,4},{7,5},{8,10},{9,11},{10,... | collective-permute-start | bytes 776 | tf_op jit(solution)/shard_map/ppermute | solution.py:118
  312.7 3.7 %collective-permute-start.2 = (f32[4,16]{0,1:T(8,128)S(1)}, f32[4,16]{0,1:T(8,128)S(1)}, u32[]{:S(2)}, u32[]{:S(2)}) collective-permute-start(f32[4,16]{0,1:T(8,128)S(1)} %add.39), channel_id=1, source_target_pairs={{0,4},{1,5},{2,6},{3,7},{4,0},{5,1},{6,2},{7,3},{8,12},{9,13},{10,... | collective-permute-start | bytes 776 | tf_op jit(solution)/shard_map/ppermute | solution.py:118
  316.3 5.2 %collective-permute-start.3 = (f32[4,16]{0,1:T(8,128)S(1)}, f32[4,16]{0,1:T(8,128)S(1)}, u32[]{:S(2)}, u32[]{:S(2)}) collective-permute-start(f32[4,16]{0,1:T(8,128)S(1)} %add.40), channel_id=1, source_target_pairs={{0,8},{1,9},{2,10},{3,11},{4,12},{5,13},{6,14},{7,15},{8,0},{9,1},... | collective-permute-start | bytes 776 | tf_op jit(solution)/shard_map/ppermute | solution.py:118
Sparse Core Ops, SparseCore 0:
  9.5 73.4 all-gather.3
  85.1 70.4 all-gather.7
  157.8 119.5 all-gather.5
